TPU v7x, 256 devices: a whole 4x4x8 slice. The times are simulated.
256 devices in a mesh: ctx: 16 (over z_lo, y), dp: 16 (over x, z_hi, core).
Axes of the slice: x: 4, y: 4, z: 8 (z_hi: 2, z_lo: 4; z = z_hi * 4 + z_lo), core: 2. Of those that a mesh axis runs over, the one named last changes fastest.
Arguments:
- inputs: bfloat16 [16, 2048, 4096], P('dp', 'ctx'), may hold values from -6 to 6
- b_proj: bfloat16 [16, 2048, 512], P('dp', 'ctx'), may hold values from -0.75 to 0.75
- c_proj: bfloat16 [16, 2048, 512], P('dp', 'ctx'), may hold values from -0.75 to 0.75
- dt_raw: float32 [16, 64, 2048], P('dp', None, 'ctx'), may hold values from -3 to 9
- a_log: float32 [64], P('dp'), may hold values from -12 to -3
- dt_bias: float32 [64], P('dp'), may hold values from 0.2 to 0.8
- d_skip: float32 [64], P('dp'), may hold values from 0.5 to 1.5
- grad_out: bfloat16 [16, 2048, 4096], P('dp', 'ctx'), may hold values from -6 to 6
Outputs:
- grad_inputs: bfloat16 [16, 2048, 4096], P('dp', 'ctx')
- grad_b: bfloat16 [16, 2048, 512], P('dp', 'ctx')
- grad_c: bfloat16 [16, 2048, 512], P('dp', 'ctx')
- grad_dt: float32 [16, 64, 2048], P('dp', None, 'ctx')
- grad_alog: float32 [64], P('dp')
- grad_bias: float32 [64], P('dp')
- grad_skip: float32 [64], P('dp')
All inputs are finite; a program needn't handle non-finite values.
Results may differ from a plain program's by a relative error of at most 0.0014.
Values sent between devices are 32-bit elements; how exact they have to be, the bound alone decides.
No kernel may reach another device: no remote copies, remote signals or barrier semaphores. Data moves between devices by JAX's collectives and lax.ppermute only.
A program may use at most 192 MiB of HBM per device.

v0:
```python
import jax
import jax.numpy as jnp
from jax import lax
from jax.sharding import PartitionSpec as P

P_SIZE = 64
N = 64
G = 8
highest = lax.Precision.HIGHEST


def slab_scan(x, b, c, raw, bias, alog, skip, state_in):
    tokens, num_heads, width = x.shape
    group_heads = num_heads // G
    dt_value = jax.nn.softplus(raw + bias[:, None])
    log_decay = dt_value * (-jnp.exp(alog))[:, None]
    cumulative = jnp.cumsum(log_decay, axis=1)
    scaled = (x * dt_value.T[:, :, None]).reshape(tokens, G, group_heads, width)
    scores = jnp.einsum("qgn,kgn->gqk", c, b, precision=highest)
    offsets = jnp.arange(tokens)
    causal = offsets[:, None] >= offsets[None, :]
    spread = cumulative[:, :, None] - cumulative[:, None, :]
    weights = jnp.where(causal, jnp.exp(jnp.where(causal, spread, 0.0)), 0.0)
    mixed = weights.reshape(G, group_heads, tokens, tokens) * scores[:, None]
    local_part = jnp.einsum("gjqk,kgjp->qgjp", mixed, scaled, precision=highest)
    tail_decay = jnp.exp(cumulative[:, -1:] - cumulative)
    weighted_b = b[:, :, None, :] * tail_decay.T.reshape(tokens, G, group_heads)[:, :, :, None]
    block_state = jnp.einsum("kgjn,kgjp->gjpn", weighted_b, scaled, precision=highest)
    block_state = block_state.reshape(num_heads, width, N)
    state_out = jnp.exp(cumulative[:, -1])[:, None, None] * state_in + block_state
    entering = state_in.reshape(G, group_heads, width, N)
    cross_part = jnp.einsum("qgn,gjpn->qgjp", c, entering, precision=highest)
    cross_part = cross_part * jnp.exp(cumulative).T.reshape(tokens, G, group_heads)[:, :, :, None]
    result = (local_part + cross_part).reshape(tokens, num_heads, width)
    result = result + skip[None, :, None] * x
    return (result, state_out)


def slab_terms(x, b, c, raw, bias, alog, grad):
    tokens, num_heads, width = x.shape
    group_heads = num_heads // G
    dt_value = jax.nn.softplus(raw + bias[:, None])
    log_decay = dt_value * (-jnp.exp(alog))[:, None]
    cumulative = jnp.cumsum(log_decay, axis=1)
    total = cumulative[:, -1]
    tail_decay = jnp.exp(total[:, None] - cumulative)
    carried = (x * (dt_value * tail_decay).T[:, :, None]).reshape(tokens, G, group_heads, width)
    local_state = jnp.einsum("tgn,tgjp->gjpn", b, carried, precision=highest)
    weighted_grad = (grad * jnp.exp(cumulative).T[:, :, None]).reshape(
        tokens, G, group_heads, width
    )
    local_source = jnp.einsum("tgn,tgjp->gjpn", c, weighted_grad, precision=highest)
    return (
        total,
        local_state.reshape(num_heads, width, N),
        local_source.reshape(num_heads, width, N),
    )


def carry_across(total, local_state, local_source):
    count = lax.axis_size("ctx")
    num_heads = total.shape[0]
    share = num_heads // count
    lanes = local_state.shape[2]
    payload = jnp.concatenate(
        [local_state, local_source, jnp.broadcast_to(total[:, None, None], (num_heads, 1, lanes))],
        axis=1,
    )
    got = lax.all_to_all(payload, "ctx", 0, 0, tiled=True)
    got = got.reshape(count, share, got.shape[1], lanes)
    width = local_state.shape[1]
    states = got[:, :, :width].reshape(count, share, width * lanes)
    sources = got[:, :, width : 2 * width].reshape(count, share, width * lanes)
    totals = got[:, :, 2 * width, 0]
    slab = jnp.arange(count)
    between = (slab[None, :, None] < slab[None, None, :]) & (
        slab[None, None, :] < slab[:, None, None]
    )
    exponent = jnp.einsum("jim,mh->jih", between.astype(jnp.float32), totals, precision=highest)
    before = slab[None, :] < slab[:, None]
    chain = jnp.where(
        before[:, :, None], jnp.exp(jnp.where(before[:, :, None], exponent, 0.0)), 0.0
    )
    entering = jnp.einsum("jih,ihx->jhx", chain, states, precision=highest)
    leaving = jnp.einsum("jkh,jhx->khx", chain, sources, precision=highest)
    back = jnp.concatenate(
        [
            entering.reshape(count * share, width, lanes),
            leaving.reshape(count * share, width, lanes),
        ],
        axis=1,
    )
    mine = lax.all_to_all(back, "ctx", 0, 0, tiled=True)
    return (mine[:, :width], mine[:, width:])


def per_device(inputs, b_proj, c_proj, dt_raw, a_log, dt_bias, d_skip, grad_out):
    params = lax.all_gather(jnp.stack([a_log, dt_bias, d_skip]), "dp", axis=1, tiled=True)
    alog_all, bias_all, skip_all = (params[0], params[1], params[2])
    tokens = inputs.shape[1]
    num_heads = alog_all.shape[0]
    x = inputs[0].astype(jnp.float32).reshape(tokens, num_heads, P_SIZE)
    grad = grad_out[0].astype(jnp.float32).reshape(tokens, num_heads, P_SIZE)
    b = b_proj[0].astype(jnp.float32).reshape(tokens, G, N)
    c = c_proj[0].astype(jnp.float32).reshape(tokens, G, N)
    raw = dt_raw[0]
    total, local_state, local_source = slab_terms(x, b, c, raw, bias_all, alog_all, grad)
    entering, leaving = carry_across(total, local_state, local_source)
    _, pullback = jax.vjp(slab_scan, x, b, c, raw, bias_all, alog_all, skip_all, entering)
    gx, gb, gc, graw, gbias, galog, gskip, _ = pullback((grad, leaving))
    grad_inputs = gx.reshape(tokens, num_heads * P_SIZE).astype(jnp.bfloat16)[None]
    grad_b = gb.reshape(tokens, G * N).astype(jnp.bfloat16)[None]
    grad_c = gc.reshape(tokens, G * N).astype(jnp.bfloat16)[None]
    grad_dt = graw[None]
    head_stats = jnp.stack([galog, gbias, gskip], axis=0)
    share_size = num_heads // lax.axis_size("dp")
    summed = lax.psum(head_stats, ("ctx", "dp"))
    own_totals = lax.dynamic_slice_in_dim(summed, lax.axis_index("dp") * share_size, share_size, 1)
    return (grad_inputs, grad_b, grad_c, grad_dt, own_totals[0], own_totals[1], own_totals[2])


def solution(mesh):
    in_specs = (
        P("dp", "ctx", None),
        P("dp", "ctx", None),
        P("dp", "ctx", None),
        P("dp", None, "ctx"),
        P("dp"),
        P("dp"),
        P("dp"),
        P("dp", "ctx", None),
    )
    out_specs = (
        P("dp", "ctx", None),
        P("dp", "ctx", None),
        P("dp", "ctx", None),
        P("dp", None, "ctx"),
        P("dp"),
        P("dp"),
        P("dp"),
    )
    return jax.shard_map(
        per_device, mesh=mesh, in_specs=in_specs, out_specs=out_specs, check_vma=False
    )
```

profile of v0, /device:TPU:1, one launch (start us, length us, event | category | flops | bytes accessed | tf_op | source)
XLA Modules:
  0.0 347.0 jit_solution(9068073911150541548)
XLA Ops:
  0.7 0.8 maximum_bitcast_fusion
  1.5 34.5 %all-gather = f32[16,4,3]{2,1,0:T(4,128)S(1)} all-gather(f32[1,4,3]{2,1,0:T(4,128)S(1)} %bitcast.241), channel_id=1, replica_groups=mesh['ctx'=16,'dp'=16] {'dp'}, dimensions={0}, use_global_device_ids=true | all-gather | bytes 816 | tf_op jit(solution)/shard_map/all_gather | solution.py:98
  36.2 0.8 copy.190
  37.6 0.7 fusion.65
  38.3 0.7 copy.198
  39.0 1.6 copy.188
  40.8 0.7 copy.194
  42.2 1.0 copy.195
  43.2 3.9 %fusion.9 = f32[8,8,64,64]{2,3,1,0:T(8,128)S(1)} fusion(bf16[128,8,64,1]{0,2,3,1:T(8,128)(2,1)S(1)} %bitcast.214, bf16[128,8,8,64]{0,3,2,1:T(8,128)(2,1)S(1)} %bitcast.198, f32[128,8,8]{0,2,1:T(8,128)} %bitcast.224), kind=kOutput, calls=%fused_computation.19 | convolution fusion | flops 403701760 | bytes 2260992 | tf_op jit(solution)/shard_map/tgn,tgjp->gjpn/dot_general | solution.py:52
  47.1 3.1 fusion.26
  50.5 3.2 pad_maximum_fusion
  53.6 5.7 %all-to-all-start = ((f32[64,129,64]{1,2,0:T(8,128)}), f32[64,129,64]{1,2,0:T(8,128)}, u32[]{:S(2)}, u32[]{:S(2)}) async-start(f32[64,129,64]{1,2,0:T(8,128)} %pad_maximum_fusion), calls=%async_computation | async-start | bytes 8388608 | tf_op jit(solution)/shard_map/all_to_all | solution.py:69
  59.4 78.3 %all-to-all-done = f32[64,129,64]{1,2,0:T(8,128)} async-done(((f32[64,129,64]{1,2,0:T(8,128)}), f32[64,129,64]{1,2,0:T(8,128)}, u32[]{:S(2)}, u32[]{:S(2)}) %all-to-all-start) | async-done | bytes 2113568 | tf_op jit(solution)/shard_map/all_to_all | solution.py:69
  137.7 1.0 slice.52
  138.7 4.9 %fusion.68 = (f32[16,4,64,64]{2,3,1,0:T(8,128)}, f32[16,4,64,64]{2,3,1,0:T(8,128)}) fusion(f32[16,4,129,64]{2,3,1,0:T(8,128)} %bitcast.26), kind=kLoop, calls=%fused_computation.110 | loop fusion | bytes 4194304 | tf_op jit(solution)/shard_map/slice | solution.py:72
  144.3 0.7 copy.205
  145.0 3.0 copy.200
  148.0 2.1 reshape.270
  150.1 1.8 convolution_bitcast_fusion.1
  151.9 0.7 copy.203
  152.6 2.4 reshape.271
  154.9 3.0 copy.204
  157.9 2.1 reshape.272
  160.0 1.8 convolution_bitcast_fusion
  161.8 0.7 copy.206
  162.5 2.3 reshape.273
  164.8 4.7 %pad_maximum_fusion.1 = f32[64,128,64]{2,1,0:T(8,128)} fusion(f32[64,64,64]{2,1,0:T(8,128)} %reshape.273, f32[64,64,64]{2,1,0:T(8,128)} %reshape.271), kind=kLoop, calls=%fused_computation.3 | loop fusion | flops 524288 | bytes 4194304 | tf_op jit(solution)/shard_map/concatenate | solution.py:86
  169.5 3.8 %copy.207 = f32[64,128,64]{1,2,0:T(8,128)} copy(f32[64,128,64]{2,1,0:T(8,128)} %pad_maximum_fusion.1) | data formatting | bytes 4194304 | tf_op jit(solution)/shard_map/concatenate | solution.py:86
  173.4 19.6 %all-to-all-start.1 = ((f32[64,128,64]{1,2,0:T(8,128)}), f32[64,128,64]{1,2,0:T(8,128)}, u32[]{:S(2)}, u32[]{:S(2)}) async-start(f32[64,128,64]{1,2,0:T(8,128)} %copy.207), calls=%async_computation.1 | async-start | bytes 4194304 | tf_op jit(solution)/shard_map/all_to_all | solution.py:93
  193.5 7.1 %fusion.11 = (f32[8,8,128]{2,1,0:T(8,128)S(1)}, f32[8,8,128]{2,1,0:T(8,128)}, f32[8,128,128]{1,2,0:T(8,128)}) fusion(f32[8,128,128]{1,2,0:T(8,128)S(1)} %fusion.72, f32[8,8,128]{2,1,0:T(8,128)S(1)} %bitcast.235, pred[128,128]{0,1:T(8,128)(4,1)S(1)} %iota_compare_fusion, bf16[8,8,64,128]{3,2,1,0:T(8,128)(2,1)S(1)} %bitcast.199, ...), kind=kOutput, calls=%fused_computation.21 | convolution fusion | flops 817741824 | bytes 3293184 | tf_op jit(solution)/shard_map/transpose(jvp(gjqk,kgjp->qgjp))/dot_general | solution.py:25
  200.8 0.9 copy.222
  201.6 6.2 %fusion.4 = f32[8,8,128,64]{2,3,1,0:T(8,128)} fusion(bf16[8,8,64,128]{3,2,1,0:T(8,128)(2,1)S(1)} %bitcast.200, f32[8,128,128]{1,2,0:T(8,128)S(1)} %fusion.72, f32[8,8,128]{2,1,0:T(8,128)S(1)} %bitcast.236, pred[128,128]{0,1:T(8,128)(4,1)S(1)} %iota_compare_fusion), kind=kOutput, calls=%fused_computation.10 | convolution fusion | flops 809500672 | bytes 3719168 | tf_op jit(solution)/shard_map/transpose(jvp(gjqk,kgjp->qgjp))/dot_general | solution.py:25
  207.8 26.7 %all-to-all-done.1 = f32[64,128,64]{1,2,0:T(8,128)} async-done(((f32[64,128,64]{1,2,0:T(8,128)}), f32[64,128,64]{1,2,0:T(8,128)}, u32[]{:S(2)}, u32[]{:S(2)}) %all-to-all-start.1) | async-done | bytes 2097184 | tf_op jit(solution)/shard_map/all_to_all | solution.py:93
  234.6 3.7 %multiply_reduce_fusion = (f32[64]{0:T(128)S(1)}, f32[64,64,64]{1,2,0:T(8,128)S(1)}, f32[64,64,64]{1,2,0:T(8,128)S(1)}) fusion(f32[64,128,64]{1,2,0:T(8,128)} %all-to-all-done.1), kind=kLoop, calls=%fused_computation.33 | loop fusion | flops 524224 | bytes 4194560 | tf_op jit(solution)/shard_map/transpose(jvp())/reduce_sum | solution.py:30
  238.3 1.8 fusion.17
  240.1 2.9 fusion.36
  243.0 3.2 fusion.19
  246.6 1.3 reduce_window_sum.25
  248.1 7.3 %multiply_reduce_fusion.1 = (f32[128,8,8]{0,2,1:T(8,128)S(1)}, f32[128,8,8,64]{0,3,2,1:T(8,128)}) fusion(f32[8,8,128,64]{2,3,1,0:T(8,128)} %fusion.4, f32[8,8,64,64]{2,3,1,0:T(8,128)} %bitcast.208, f32[128,8,8]{0,2,1:T(8,128)S(1)} %bitcast.227, f32[128,8,64]{0,2,1:T(8,128)S(1)} %convert_element_type.70, bf16[128,8,8,64]{0,3,2,1:T(8,128)(2,1)S(1)} %bitcast.206), kind=kOutput, calls=%fused_computation.34 | convolution fusion | flops 405266432 | bytes 6619136 | tf_op jit(solution)/shard_map/transpose(jvp(kgjn,kgjp->gjpn))/dot_general | solution.py:28
  255.5 0.7 fusion.66
  256.3 2.5 fusion.16
  259.1 80.5 %psum.7 = f32[3,64]{1,0:T(4,128)S(1)} all-reduce(f32[3,64]{1,0:T(4,128)S(1)} %pad_maximum_fusion.2), channel_id=1, replica_groups=mesh['ctx'=16,'dp'=16] {'ctx','dp'}, use_global_device_ids=true, to_apply=%region_15.16 | all-reduce | flops 192 | bytes 1536 | tf_op jit(solution)/shard_map/psum | solution.py:117
  340.2 1.5 fusion.40
  341.7 0.8 copy.228
  342.5 1.8 fusion.39
  344.2 0.8 copy.227
  345.0 1.3 copy.226
  346.3 0.7 copy.229
  (77 shorter events, 4.5 us)
Async XLA Ops:
  0.6 40.0 %copy-start.11 = (bf16[1,128,512]{2,1,0:T(8,128)(2,1)S(1)}, bf16[1,128,512]{2,1,0:T(8,128)(2,1)}, u32[]{:S(2)}) copy-start(bf16[1,128,512]{2,1,0:T(8,128)(2,1)} %param.10) | copy-start | bytes 393220
  0.6 40.8 %copy-start.1 = (bf16[1,128,4096]{2,1,0:T(8,128)(2,1)S(1)}, bf16[1,128,4096]{2,1,0:T(8,128)(2,1)}, u32[]{:S(2)}) copy-start(bf16[1,128,4096]{2,1,0:T(8,128)(2,1)} %param.8) | copy-start | bytes 3145732
  36.2 0.9 copy-start.16
  36.2 0.9 copy-start.18
  36.2 2.8 copy-start.14
  37.5 1.5 copy-start.9
  37.6 12.6 %copy-start.12 = (f32[64]{0:T(128)}, f32[64]{0:T(128)S(1)}, u32[]{:S(2)}) copy-start(f32[64]{0:T(128)S(1)} %slice_bitcast_fusion.5) | copy-start | bytes 772
  42.2 4.9 %copy-start.8 = (f32[128,64]{0,1:T(8,128)S(1)}, f32[128,64]{0,1:T(8,128)}, u32[]{:S(2)}) copy-start(f32[128,64]{0,1:T(8,128)} %copy.194) | copy-start | bytes 98308
  53.6 84.1 %all-to-all-start = ((f32[64,129,64]{1,2,0:T(8,128)}), f32[64,129,64]{1,2,0:T(8,128)}, u32[]{:S(2)}, u32[]{:S(2)}) async-start(f32[64,129,64]{1,2,0:T(8,128)} %pad_maximum_fusion), calls=%async_computation | async-start | bytes 8388608 | tf_op jit(solution)/shard_map/all_to_all | solution.py:69
  173.4 19.6 %copy-start.6 = (f32[128,64]{1,0:T(8,128)S(1)}, f32[128,64]{1,0:T(8,128)}, u32[]{:S(2)}) copy-start(f32[128,64]{1,0:T(8,128)} %get-tuple-element.71) | copy-start | bytes 98308
  173.4 19.7 %copy-start.5 = (f32[128,64]{1,0:T(8,128)S(1)}, f32[128,64]{1,0:T(8,128)}, u32[]{:S(2)}) copy-start(f32[128,64]{1,0:T(8,128)} %get-tuple-element.73) | copy-start | bytes 98308
  173.4 20.1 %copy-start.10 = (f32[64,128]{1,0:T(8,128)S(1)}, f32[64,128]{1,0:T(8,128)}, u32[]{:S(2)}) copy-start(f32[64,128]{1,0:T(8,128)} %copy-done.9) | copy-start | bytes 98308
  173.4 61.2 %all-to-all-start.1 = ((f32[64,128,64]{1,2,0:T(8,128)}), f32[64,128,64]{1,2,0:T(8,128)}, u32[]{:S(2)}, u32[]{:S(2)}) async-start(f32[64,128,64]{1,2,0:T(8,128)} %copy.207), calls=%async_computation.1 | async-start | bytes 4194304 | tf_op jit(solution)/shard_map/all_to_all | solution.py:93
  193.1 50.0 %copy-start.3 = (f32[128,64]{0,1:T(8,128)}, f32[128,64]{0,1:T(8,128)S(1)}, u32[]{:S(2)}) copy-start(f32[128,64]{0,1:T(8,128)S(1)} %copy.212) | copy-start | bytes 98308
  238.3 4.8 %copy-start = (f32[64,64,64]{1,2,0:T(8,128)}, f32[64,64,64]{1,2,0:T(8,128)S(1)}, u32[]{:S(2)}) copy-start(f32[64,64,64]{1,2,0:T(8,128)S(1)} %get-tuple-element.67) | copy-start | bytes 3145732
  238.3 1.8 copy-start.2
  243.0 3.3 copy-start.13
  248.0 7.4 %copy-start.15 = (f32[64]{0:T(128)S(1)}, f32[64]{0:T(128)}, u32[]{:S(2)}) copy-start(f32[64]{0:T(128)} %copy-done.14) | copy-start | bytes 772
  248.0 7.4 %copy-start.19 = (f32[64]{0:T(128)S(1)}, f32[64]{0:T(128)}, u32[]{:S(2)}) copy-start(f32[64]{0:T(128)} %copy-done.18) | copy-start | bytes 772
  248.0 8.1 %copy-start.17 = (f32[64,3]{0,1:T(4,128)S(1)}, f32[64,3]{0,1:T(4,128)}, u32[]{:S(2)}) copy-start(f32[64,3]{0,1:T(4,128)} %copy-done.16) | copy-start | bytes 2308
  248.0 8.3 %copy-start.4 = (f32[128,64]{0,1:T(8,128)S(1)}, f32[128,64]{0,1:T(8,128)}, u32[]{:S(2)}) copy-start(f32[128,64]{0,1:T(8,128)} %copy-done.3) | copy-start | bytes 98308
  341.7 4.6 %copy-start.7 = (f32[64,128]{0,1:T(8,128)S(1)}, f32[64,128]{0,1:T(8,128)}, u32[]{:S(2)}) copy-start(f32[64,128]{0,1:T(8,128)} %get-tuple-element.62) | copy-start | bytes 98308
where the time goes:
time: 348 us; the launch traced here: 347 us
  blocking collectives  115 us (33%)
  waiting for transfers between devices  105 us (30%)
  matrix products  43.3 us (12%)
  local copies, waits for them, and re-layouts  38.9 us (11%)
  starting transfers between devices  25.3 us (7%)
  other arithmetic  18.2 us (5%)
    psum x1, blocking collectives, per_device(): summed = lax.psum(head_stats, ('ctx', 'dp'))  80.5 us
    all_to_all x1, waiting for transfers between devices, carry_across(): got = lax.all_to_all(payload, 'ctx', 0, 0, tiled=True)  78.3 us
    all_gather x1, blocking collectives, per_device(): lax.all_gather(jnp.stack([a_log, dt_bias, d_skip]), 'dp', axis=1, tiled=T...  34.5 us
    all_to_all x1, waiting for transfers between devices, carry_across(): mine = lax.all_to_all(back, 'ctx', 0, 0, tiled=True)  26.7 us
    all_to_all x1, starting transfers between devices, carry_across(): mine = lax.all_to_all(back, 'ctx', 0, 0, tiled=True)  19.6 us
    dot_general x2, matrix products, slab_scan(): local_part = jnp.einsum('gjqk,kgjp->qgjp', mixed, scaled, precision=highest)  13.3 us
    dot_general x2, matrix products, slab_scan(): jnp.einsum('kgjn,kgjp->gjpn', weighted_b, scaled, precision=highest)  10.5 us
    unnamed x51, local copies, waits for them, and re-layouts  8.07 us
  transfers between devices with their start and end apart: 2, of which 2 were waited for; matrix products, arithmetic and copies ran while one was open for 4% of the time, Pallas kernels for 0%

commit v1 on v0

--- a/solution.py
+++ b/solution.py
@@ -114,7 +114,7 @@
     grad_dt = graw[None]
     head_stats = jnp.stack([galog, gbias, gskip], axis=0)
     share_size = num_heads // lax.axis_size("dp")
-    summed = lax.psum(head_stats, ("ctx", "dp"))
+    summed = jnp.sum(lax.all_gather(head_stats, ("ctx", "dp")), axis=0)
     own_totals = lax.dynamic_slice_in_dim(summed, lax.axis_index("dp") * share_size, share_size, 1)
     return (grad_inputs, grad_b, grad_c, grad_dt, own_totals[0], own_totals[1], own_totals[2])
 

time: 348 us -> 678 us (1.95)
  the two profiles are of different devices: /device:TPU:1 before, /device:TPU:193 now
where the time goes in v1:
time: 678 us; the launch traced here: 672 us
  blocking collectives  432 us (64%)
  waiting for transfers between devices  126 us (19%)
  matrix products  42.3 us (6%)
  local copies, waits for them, and re-layouts  38.9 us (6%)
  other arithmetic  18.5 us (3%)
  starting transfers between devices  13 us (2%)
    all_gather x1, blocking collectives, per_device(): summed = jnp.sum(lax.all_gather(head_stats, ('ctx', 'dp')), axis=0)  407 us
    all_to_all x1, waiting for transfers between devices, carry_across(): got = lax.all_to_all(payload, 'ctx', 0, 0, tiled=True)  93.1 us
    all_to_all x1, waiting for transfers between devices, carry_across(): mine = lax.all_to_all(back, 'ctx', 0, 0, tiled=True)  32.4 us
    all_gather x1, blocking collectives, per_device(): lax.all_gather(jnp.stack([a_log, dt_bias, d_skip]), 'dp', axis=1, tiled=T...  24.9 us
  transfers between devices with their start and end apart: 2, of which 2 were waited for; matrix products, arithmetic and copies ran while one was open for 2% of the time, Pallas kernels for 0%

profile of v1, /device:TPU:193, one launch (start us, length us, event | category | flops | bytes accessed | tf_op | source)
XLA Modules:
  0.0 671.5 jit_solution(7891102443150185500)
XLA Ops:
  0.7 0.8 maximum_bitcast_fusion
  1.5 24.9 %all-gather.1 = f32[16,4,3]{2,1,0:T(4,128)S(1)} all-gather(f32[1,4,3]{2,1,0:T(4,128)S(1)} %bitcast.243), channel_id=1, replica_groups=mesh['ctx'=16,'dp'=16] {'dp'}, dimensions={0}, use_global_device_ids=true | all-gather | bytes 816 | tf_op jit(solution)/shard_map/all_gather | solution.py:98
  26.6 0.8 copy.190
  28.0 0.7 fusion.65
  28.7 0.7 copy.198
  29.4 1.6 copy.188
  31.2 0.7 copy.194
  31.9 0.7 copy.189
  32.6 1.0 copy.195
  33.6 3.9 fusion.9
  37.5 3.1 fusion.26
  40.9 3.2 pad_maximum_fusion
  44.1 8.3 %all-to-all-start = ((f32[64,129,64]{1,2,0:T(8,128)}), f32[64,129,64]{1,2,0:T(8,128)}, u32[]{:S(2)}, u32[]{:S(2)}) async-start(f32[64,129,64]{1,2,0:T(8,128)} %pad_maximum_fusion), calls=%async_computation | async-start | bytes 8388608 | tf_op jit(solution)/shard_map/all_to_all | solution.py:69
  52.3 93.1 %all-to-all-done = f32[64,129,64]{1,2,0:T(8,128)} async-done(((f32[64,129,64]{1,2,0:T(8,128)}), f32[64,129,64]{1,2,0:T(8,128)}, u32[]{:S(2)}, u32[]{:S(2)}) %all-to-all-start) | async-done | bytes 2113568 | tf_op jit(solution)/shard_map/all_to_all | solution.py:69
  145.4 1.0 slice.52
  146.4 4.9 fusion.68
  152.0 0.7 copy.205
  152.7 3.0 copy.200
  155.6 2.1 reshape.270
  157.8 1.8 convolution_bitcast_fusion.1
  159.6 0.7 copy.203
  160.3 2.4 reshape.271
  162.6 3.0 copy.204
  165.6 2.1 reshape.272
  167.7 1.8 convolution_bitcast_fusion
  169.5 0.7 copy.206
  170.2 2.3 reshape.273
  172.5 4.7 pad_maximum_fusion.1
  177.2 3.8 copy.207
  181.0 4.7 all-to-all-start.1
  186.3 7.1 %fusion.11 = (f32[8,8,128]{2,1,0:T(8,128)S(1)}, f32[8,8,128]{2,1,0:T(8,128)}, f32[8,128,128]{1,2,0:T(8,128)}) fusion(f32[8,128,128]{1,2,0:T(8,128)S(1)} %fusion.72, f32[8,8,128]{2,1,0:T(8,128)S(1)} %bitcast.237, pred[128,128]{0,1:T(8,128)(4,1)S(1)} %iota_compare_fusion, bf16[8,8,64,128]{3,2,1,0:T(8,128)(2,1)S(1)} %bitcast.201, ...), kind=kOutput, calls=%fused_computation.21 | convolution fusion | flops 817741824 | bytes 3293184 | tf_op jit(solution)/shard_map/transpose(jvp(gjqk,kgjp->qgjp))/dot_general | solution.py:25
  193.5 0.9 copy.222
  194.4 6.3 fusion.4
  200.7 32.4 %all-to-all-done.1 = f32[64,128,64]{1,2,0:T(8,128)} async-done(((f32[64,128,64]{1,2,0:T(8,128)}), f32[64,128,64]{1,2,0:T(8,128)}, u32[]{:S(2)}, u32[]{:S(2)}) %all-to-all-start.1) | async-done | bytes 2097184 | tf_op jit(solution)/shard_map/all_to_all | solution.py:93
  233.2 3.7 multiply_reduce_fusion
  236.9 1.8 fusion.17
  238.7 2.9 fusion.36
  241.6 3.2 fusion.19
  245.3 1.3 reduce_window_sum.25
  246.7 7.3 %multiply_reduce_fusion.1 = (f32[128,8,8]{0,2,1:T(8,128)S(1)}, f32[128,8,8,64]{0,3,2,1:T(8,128)}) fusion(f32[8,8,128,64]{2,3,1,0:T(8,128)} %fusion.4, f32[8,8,64,64]{2,3,1,0:T(8,128)} %bitcast.210, f32[128,8,8]{0,2,1:T(8,128)S(1)} %bitcast.229, f32[128,8,64]{0,2,1:T(8,128)S(1)} %convert_element_type.70, bf16[128,8,8,64]{0,3,2,1:T(8,128)(2,1)S(1)} %bitcast.208), kind=kOutput, calls=%fused_computation.34 | convolution fusion | flops 405266432 | bytes 6619136 | tf_op jit(solution)/shard_map/transpose(jvp(kgjn,kgjp->gjpn))/dot_general | solution.py:28
  254.0 0.7 fusion.66
  254.9 2.5 fusion.16
  257.7 407.0 %all-gather.2 = f32[256,3,64]{2,1,0:T(4,128)S(1)} all-gather(f32[1,3,64]{2,1,0:T(4,128)S(1)} %maximum_bitcast_fusion.1), channel_id=2, replica_groups=mesh['ctx'=16,'dp'=16] {'ctx','dp'}, dimensions={0}, use_global_device_ids=true | all-gather | bytes 197376 | tf_op jit(solution)/shard_map/all_gather | solution.py:117
  665.6 1.5 fusion.40
  667.1 0.8 copy.228
  668.5 0.8 copy.227
  669.3 1.3 copy.226
  670.6 0.7 copy.229
  (82 shorter events, 4.7 us)
Async XLA Ops:
  0.6 30.4 %copy-start.13 = (bf16[1,128,512]{2,1,0:T(8,128)(2,1)S(1)}, bf16[1,128,512]{2,1,0:T(8,128)(2,1)}, u32[]{:S(2)}) copy-start(bf16[1,128,512]{2,1,0:T(8,128)(2,1)} %param.10) | copy-start | bytes 393220
  0.6 31.3 %copy-start.3 = (bf16[1,128,4096]{2,1,0:T(8,128)(2,1)S(1)}, bf16[1,128,4096]{2,1,0:T(8,128)(2,1)}, u32[]{:S(2)}) copy-start(bf16[1,128,4096]{2,1,0:T(8,128)(2,1)} %param.8) | copy-start | bytes 3145732
  26.6 0.9 copy-start.18
  26.6 0.9 copy-start.20
  26.6 2.8 copy-start.16
  27.9 1.5 copy-start.11
  28.0 12.6 %copy-start.14 = (f32[64]{0:T(128)}, f32[64]{0:T(128)S(1)}, u32[]{:S(2)}) copy-start(f32[64]{0:T(128)S(1)} %slice_bitcast_fusion.5) | copy-start | bytes 772
  32.6 4.9 copy-start.10
  44.1 101.3 %all-to-all-start = ((f32[64,129,64]{1,2,0:T(8,128)}), f32[64,129,64]{1,2,0:T(8,128)}, u32[]{:S(2)}, u32[]{:S(2)}) async-start(f32[64,129,64]{1,2,0:T(8,128)} %pad_maximum_fusion), calls=%async_computation | async-start | bytes 8388608 | tf_op jit(solution)/shard_map/all_to_all | solution.py:69
  181.0 4.7 copy-start.8
  181.0 4.8 copy-start.7
  181.0 5.2 copy-start.12
  181.0 52.2 %all-to-all-start.1 = ((f32[64,128,64]{1,2,0:T(8,128)}), f32[64,128,64]{1,2,0:T(8,128)}, u32[]{:S(2)}, u32[]{:S(2)}) async-start(f32[64,128,64]{1,2,0:T(8,128)} %copy.207), calls=%async_computation.1 | async-start | bytes 4194304 | tf_op jit(solution)/shard_map/all_to_all | solution.py:93
  185.8 55.8 %copy-start.5 = (f32[128,64]{0,1:T(8,128)}, f32[128,64]{0,1:T(8,128)S(1)}, u32[]{:S(2)}) copy-start(f32[128,64]{0,1:T(8,128)S(1)} %copy.212) | copy-start | bytes 98308
  236.9 4.8 copy-start
  236.9 1.8 copy-start.4
  241.6 3.3 copy-start.15
  246.6 7.4 %copy-start.17 = (f32[64]{0:T(128)S(1)}, f32[64]{0:T(128)}, u32[]{:S(2)}) copy-start(f32[64]{0:T(128)} %copy-done.16) | copy-start | bytes 772
  246.6 7.4 %copy-start.21 = (f32[64]{0:T(128)S(1)}, f32[64]{0:T(128)}, u32[]{:S(2)}) copy-start(f32[64]{0:T(128)} %copy-done.20) | copy-start | bytes 772
  246.6 8.1 %copy-start.19 = (f32[64,3]{0,1:T(4,128)S(1)}, f32[64,3]{0,1:T(4,128)}, u32[]{:S(2)}) copy-start(f32[64,3]{0,1:T(4,128)} %copy-done.18) | copy-start | bytes 2308
  246.7 8.2 %copy-start.6 = (f32[128,64]{0,1:T(8,128)S(1)}, f32[128,64]{0,1:T(8,128)}, u32[]{:S(2)}) copy-start(f32[128,64]{0,1:T(8,128)} %copy-done.5) | copy-start | bytes 98308
  257.4 410.4 %copy-start.1 = (f32[8,128,128]{1,2,0:T(8,128)S(1)}, f32[8,128,128]{1,2,0:T(8,128)}, u32[]{:S(2)}) copy-start(f32[8,128,128]{1,2,0:T(8,128)} %get-tuple-element.58) | copy-start | bytes 1572868
  257.4 410.4 %copy-start.2 = (f32[128,8,64]{0,2,1:T(8,128)S(1)}, f32[128,8,64]{0,2,1:T(8,128)}, u32[]{:S(2)}) copy-start(f32[128,8,64]{0,2,1:T(8,128)} %get-tuple-element.60) | copy-start | bytes 786436
  667.1 3.5 copy-start.9
